TPU v7x, 32 devices: a whole 2x2x4 slice. The times are simulated.
32 devices in a mesh: gx: 8 (over z, x), ka: 4 (over y, core).
Axes of the slice: x: 2, y: 2, z: 4, core: 2. Of those that a mesh axis runs over, the one named last changes fastest.
Arguments:
- direct_snapshots: bfloat16 [128, 32, 64, 128], P('ka', 'gx'), may hold values from -40 to 40
- adjoint_snapshots: bfloat16 [128, 32, 64, 128], P('ka', 'gx'), may hold values from -40 to 40
- quad_weight: float32 [32, 64], P('gx'), may hold values from 0.5 to 2
- mean_velocity: float32 [32, 64], P('gx'), may hold values from 0.2 to 1.2
- diffusivity: float32 [32, 64], P('gx'), may hold values from 0.05 to 0.5
Outputs:
- hankel_gram: float32 [8192, 128], P(('ka', 'gx'))
- reduced_operator: float32 [8192, 128], P(('ka', 'gx'))
- hankel_norm: float32 [128], P('ka')
All inputs are finite; a program needn't handle non-finite values.
Results may differ from a plain program's by a relative error of at most 0.0071.
Values may be sent and summed in bfloat16 or wider, within the bound.
No kernel may reach another device: no remote copies, remote signals or barrier semaphores. Data moves between devices by JAX's collectives and lax.ppermute only.
A program may use at most 64 MiB of HBM per device.

v0:
```python
import math
import jax
import jax.numpy as jnp
from jax import lax
from jax.sharding import PartitionSpec as P

epsilon = 1e-06


def padded_2(cells, sides, width):
    for axis, dim in sides:
        count = lax.axis_size(axis)
        ends = count - 1
        head = lax.slice_in_dim(cells, 0, width, axis=dim)
        tail = lax.slice_in_dim(cells, cells.shape[dim] - width, cells.shape[dim], axis=dim)
        cells = jnp.concatenate(
            [
                lax.ppermute(tail, axis, [(i, (i + 1) % count) for i in range(ends)]),
                cells,
                lax.ppermute(head, axis, [((i + 1) % count, i) for i in range(ends)]),
            ],
            axis=dim,
        )
    return cells


def dft_tables(count):
    wave_index = jnp.arange(count, dtype=jnp.int32) - count // 2
    angle_index = jnp.arange(count, dtype=jnp.int32)
    residues = wave_index[:, None] * angle_index[None, :] % count
    phases = 2.0 * math.pi * residues.astype(jnp.float32) / count
    scaling = 1.0 / math.sqrt(count)
    return (
        (jnp.cos(phases) * scaling).astype(jnp.bfloat16),
        (jnp.sin(phases) * scaling).astype(jnp.bfloat16),
    )


def combine_parts(cos_part, sin_part, half):
    real_part = cos_part[..., :half] + sin_part[..., half:]
    imag_part = cos_part[..., half:] - sin_part[..., :half]
    return jnp.concatenate([real_part, imag_part], axis=-1).astype(jnp.bfloat16)


def complex_blocks(product, half):
    upper_rows = product[..., :half, :]
    lower_rows = product[..., half:, :]
    pieces = []
    for offset in (0, 2 * half):
        pieces.append(
            upper_rows[..., offset : offset + half]
            + lower_rows[..., offset + half : offset + 2 * half]
        )
        pieces.append(
            upper_rows[..., offset + half : offset + 2 * half]
            - lower_rows[..., offset : offset + half]
        )
    return jnp.concatenate(pieces, axis=-1)


def local(direct_snapshots, adjoint_snapshots, quad_weight, mean_velocity, diffusivity):
    local_angles, axial_cells, radial_cells, columns = direct_snapshots.shape
    snap_count = columns // 2
    total_angles = local_angles * lax.axis_size("ka")
    cos_table, sin_table = dft_tables(total_angles)
    first_wave = lax.axis_index("ka") * local_angles
    moved_direct, moved_adjoint = (
        lax.all_to_all(direct_snapshots, "ka", split_axis=2, concat_axis=0, tiled=True),
        lax.all_to_all(adjoint_snapshots, "ka", split_axis=2, concat_axis=0, tiled=True),
    )

    def transform_all(snapshots):
        flattened = snapshots.reshape(total_angles, -1)
        cos_part = jnp.dot(cos_table, flattened, preferred_element_type=jnp.float32).reshape(
            snapshots.shape
        )
        sin_part = jnp.dot(sin_table, flattened, preferred_element_type=jnp.float32).reshape(
            snapshots.shape
        )
        return combine_parts(cos_part, sin_part, snap_count)

    direct_modes, adjoint_modes = (
        lax.all_to_all(transform_all(moved_direct), "ka", split_axis=0, concat_axis=2, tiled=True),
        lax.all_to_all(transform_all(moved_adjoint), "ka", split_axis=0, concat_axis=2, tiled=True),
    )
    padded = padded_2(direct_modes, (("gx", 1),), 1)
    field_f32 = direct_modes.astype(jnp.float32)
    forward = padded[:, 2:].astype(jnp.float32)
    behind = padded[:, :-2].astype(jnp.float32)
    radial_pad = jnp.pad(field_f32, ((0, 0), (0, 0), (1, 1), (0, 0)))
    outward = radial_pad[:, :, 2:]
    inward = radial_pad[:, :, :-2]
    radius = 0.25 + (jnp.arange(radial_cells, dtype=jnp.float32) + 0.5) / radial_cells
    wavenumber = (
        first_wave + jnp.arange(local_angles, dtype=jnp.int32) - total_angles // 2
    ).astype(jnp.float32) / total_angles
    azimuthal = (wavenumber[:, None] / radius[None, :]) ** 2
    velocity = mean_velocity[None, :, :, None]
    diffusion = diffusivity[None, :, :, None]
    image = (
        -velocity * (forward - behind) * 0.5
        + diffusion
        * (
            forward
            + behind
            + outward
            + inward
            - 4.0 * field_f32
            - azimuthal[:, None, :, None] * field_f32
        )
    ).astype(jnp.bfloat16)
    norm_factor = 1.0 / math.sqrt(axial_cells * lax.axis_size("gx") * radial_cells)
    plane_weight = quad_weight * norm_factor
    weighted = (adjoint_modes.astype(jnp.float32) * plane_weight[None, :, :, None]).astype(
        jnp.bfloat16
    )
    right_side = jnp.concatenate([direct_modes, image], axis=-1)
    product = jnp.einsum(
        "kpa,kpb->kab",
        weighted.reshape(local_angles, -1, columns),
        right_side.reshape(local_angles, -1, 2 * columns),
        preferred_element_type=jnp.float32,
    )
    gram_terms = complex_blocks(product, snap_count).reshape(local_angles * snap_count, 2 * columns)
    row_count = gram_terms.shape[0] // lax.axis_size("gx")
    row_index = lax.axis_index("gx") * row_count + jnp.arange(row_count, dtype=jnp.int32)
    owner = row_index // snap_count
    selector = (owner[:, None] == jnp.arange(local_angles, dtype=jnp.int32)[None, :]).astype(
        jnp.float32
    )
    own_rows = lax.psum_scatter(gram_terms, "gx", scatter_dimension=0, tiled=True)
    row_energy = jnp.sum(own_rows[:, :columns] ** 2, axis=1)
    energy = lax.psum(jnp.sum(selector * row_energy[:, None], axis=0), "gx")
    mean_sq = energy / (2.0 * snap_count * snap_count)
    row_scale = jnp.sum(selector * lax.rsqrt(mean_sq + epsilon)[None, :], axis=1)
    hankel_gram = own_rows[:, :columns] * row_scale[:, None]
    reduced_operator = own_rows[:, columns:] * row_scale[:, None]
    hankel_norm = jnp.sqrt(mean_sq)
    return (hankel_gram, reduced_operator, hankel_norm)


def permuted_tables(count, wave_index):
    angle_index = jnp.arange(count, dtype=jnp.int32)
    residues = wave_index[:, None] * angle_index[None, :] % count
    phases = 2.0 * math.pi * residues.astype(jnp.float32) / count
    scaling = 1.0 / math.sqrt(count)
    return (
        (jnp.cos(phases) * scaling).astype(jnp.bfloat16),
        (jnp.sin(phases) * scaling).astype(jnp.bfloat16),
    )


def by_wavenumber(direct_snapshots, adjoint_snapshots, quad_weight, mean_velocity, diffusivity):
    local_angles, axial_cells, radial_cells, columns = direct_snapshots.shape
    snap_count = columns // 2
    band_count = lax.axis_size("ka")
    axial_count = lax.axis_size("gx")
    total_angles = local_angles * band_count
    devices = band_count * axial_count
    waves_here = total_angles // devices
    points = axial_cells * radial_cells
    band = points // band_count
    band_index = lax.axis_index("ka")
    axial_index = lax.axis_index("gx")
    row = jnp.arange(total_angles, dtype=jnp.int32)
    chunk = row // waves_here
    owner = chunk % band_count * axial_count + chunk // band_count
    wave_index = owner * waves_here + row % waves_here - total_angles // 2
    cos_table, sin_table = permuted_tables(total_angles, wave_index)
    fields = jnp.stack([mean_velocity, diffusivity])
    fields = lax.all_gather(fields, "gx", axis=1, tiled=True)

    def gather_angles(snapshots):
        flat = snapshots.reshape(local_angles, points, columns)
        return lax.all_to_all(flat, "ka", split_axis=1, concat_axis=0, tiled=True)

    def transform_all(moved):
        flattened = moved.reshape(total_angles, -1)
        cos_part = jnp.dot(cos_table, flattened, preferred_element_type=jnp.float32).reshape(
            moved.shape
        )
        sin_part = jnp.dot(sin_table, flattened, preferred_element_type=jnp.float32).reshape(
            moved.shape
        )
        return combine_parts(cos_part, sin_part, snap_count)

    def scatter_waves(modes):
        return lax.all_to_all(modes, ("gx", "ka"), split_axis=0, concat_axis=1, tiled=True)

    direct_modes = scatter_waves(transform_all(gather_angles(direct_snapshots)))
    norm_factor = 1.0 / math.sqrt(axial_cells * axial_count * radial_cells)
    plane_weight = (quad_weight * norm_factor).reshape(points)
    band_weight = lax.dynamic_slice_in_dim(plane_weight, band_index * band, band)
    adjoint_modes = transform_all(gather_angles(adjoint_snapshots))
    weighted = (adjoint_modes.astype(jnp.float32) * band_weight[None, :, None]).astype(jnp.bfloat16)
    weighted = scatter_waves(weighted)
    all_axial = axial_cells * axial_count
    field = direct_modes.reshape(waves_here, all_axial, radial_cells, columns)
    field_f32 = field.astype(jnp.float32)
    padded = jnp.pad(field_f32, ((0, 0), (1, 1), (1, 1), (0, 0)))
    forward = padded[:, 2:, 1:-1]
    behind = padded[:, :-2, 1:-1]
    outward = padded[:, 1:-1, 2:]
    inward = padded[:, 1:-1, :-2]
    radius = 0.25 + (jnp.arange(radial_cells, dtype=jnp.float32) + 0.5) / radial_cells
    first_wave = (band_index * axial_count + axial_index) * waves_here
    wavenumber = (first_wave + jnp.arange(waves_here, dtype=jnp.int32) - total_angles // 2).astype(
        jnp.float32
    ) / total_angles
    azimuthal = (wavenumber[:, None] / radius[None, :]) ** 2
    velocity = fields[0][None, :, :, None]
    diffusion = fields[1][None, :, :, None]
    image = (
        -velocity * (forward - behind) * 0.5
        + diffusion
        * (
            forward
            + behind
            + outward
            + inward
            - 4.0 * field_f32
            - azimuthal[:, None, :, None] * field_f32
        )
    ).astype(jnp.bfloat16)
    right_side = jnp.concatenate([field, image], axis=-1)
    product = jnp.einsum(
        "kpa,kpb->kab",
        weighted,
        right_side.reshape(waves_here, -1, 2 * columns),
        preferred_element_type=jnp.float32,
    )
    gram_terms = complex_blocks(product, snap_count)
    energy = jnp.sum(gram_terms[..., :columns] ** 2, axis=(1, 2))
    mean_sq = energy / (2.0 * snap_count * snap_count)
    scales = lax.rsqrt(mean_sq + epsilon)
    hankel_gram = (gram_terms[..., :columns] * scales[:, None, None]).reshape(-1, columns)
    reduced_operator = (gram_terms[..., columns:] * scales[:, None, None]).reshape(-1, columns)
    hankel_norm = lax.all_gather(jnp.sqrt(mean_sq), "gx", tiled=True)
    return (hankel_gram, reduced_operator, hankel_norm)


def dispatch(direct_snapshots, *rest):
    local_angles, axial_cells, radial_cells, _ = direct_snapshots.shape
    band_count = lax.axis_size("ka")
    devices = band_count * lax.axis_size("gx")
    whole_waves = local_angles * band_count % devices == 0
    even_bands = axial_cells * radial_cells % band_count == 0
    body = by_wavenumber if whole_waves and even_bands else local
    return body(direct_snapshots, *rest)


def solution(mesh):
    placed = (
        P("ka", "gx", None, None),
        P("ka", "gx", None, None),
        P("gx", None),
        P("gx", None),
        P("gx", None),
    )
    return jax.shard_map(
        dispatch,
        mesh=mesh,
        in_specs=placed,
        out_specs=(P(("ka", "gx"), None), P(("ka", "gx"), None), P("ka")),
        check_vma=False,
    )
```

profile of v0, /device:TPU:0, one launch (start us, length us, event | category | flops | bytes accessed | tf_op | source)
XLA Modules:
  0.0 225.0 jit_solution(7960492328090820535)
XLA Ops:
  0.6 4.3 %copy.30 = bf16[32,4,64,128]{3,0,2,1:T(8,128)(2,1)} copy(bf16[32,4,64,128]{3,2,1,0:T(8,128)(2,1)} %param.6) | data formatting | bytes 4194304 | tf_op args[1]
  4.9 4.2 %all-to-all-start = ((bf16[32,256,128]{2,0,1:T(8,128)(2,1)}), bf16[32,256,128]{2,0,1:T(8,128)(2,1)S(1)}, u32[]{:S(2)}, u32[]{:S(2)}) async-start(bf16[32,256,128]{2,0,1:T(8,128)(2,1)} %bitcast.66), calls=%async_computation | async-start | bytes 4194304 | tf_op jit(solution)/shard_map/all_to_all | solution.py:175
  9.1 4.3 %copy.36 = bf16[32,4,64,128]{3,0,2,1:T(8,128)(2,1)} copy(bf16[32,4,64,128]{3,2,1,0:T(8,128)(2,1)} %param.5) | data formatting | bytes 4194304 | tf_op args[0]
  13.4 21.4 %all-to-all-done = bf16[32,256,128]{2,0,1:T(8,128)(2,1)S(1)} async-done(((bf16[32,256,128]{2,0,1:T(8,128)(2,1)}), bf16[32,256,128]{2,0,1:T(8,128)(2,1)S(1)}, u32[]{:S(2)}, u32[]{:S(2)}) %all-to-all-start) | async-done | bytes 2097184 | tf_op jit(solution)/shard_map/all_to_all | solution.py:175
  34.8 4.4 %all-to-all-start.2 = ((bf16[32,256,128]{2,0,1:T(8,128)(2,1)}), bf16[32,256,128]{2,0,1:T(8,128)(2,1)}, u32[]{:S(2)}, u32[]{:S(2)}) async-start(bf16[32,256,128]{2,0,1:T(8,128)(2,1)} %bitcast.11), calls=%async_computation.2 | async-start | bytes 4194304 | tf_op jit(solution)/shard_map/all_to_all | solution.py:175
  40.3 3.1 %copy.51 = bf16[16,8,64,128]{3,1,2,0:T(8,128)(2,1)} copy(bf16[16,8,64,128]{3,2,1,0:T(8,128)(2,1)S(1)} %bitcast.67) | data formatting | bytes 4194304
  43.4 3.2 %copy.33 = bf16[8192,128]{1,0:T(8,128)(2,1)S(1)} copy(bf16[8192,128]{0,1:T(8,128)(2,1)} %bitcast.68) | data formatting | bytes 4194304 | tf_op jit(solution)/shard_map/dot_general | solution.py:179
  47.6 1.0 fusion.26
  48.6 1.0 fusion.10
  50.1 2.8 %copy.34 = bf16[128,64,128]{2,1,0:T(8,128)(2,1)} copy(bf16[128,64,128]{0,2,1:T(8,128)(2,1)S(1)} %multiply_convert_fusion) | data formatting | bytes 4194304 | tf_op jit(solution)/shard_map/convert_element_type | solution.py:195
  53.0 12.1 %all-to-all-done.2 = bf16[32,256,128]{2,0,1:T(8,128)(2,1)} async-done(((bf16[32,256,128]{2,0,1:T(8,128)(2,1)}), bf16[32,256,128]{2,0,1:T(8,128)(2,1)}, u32[]{:S(2)}, u32[]{:S(2)}) %all-to-all-start.2) | async-done | bytes 2097184 | tf_op jit(solution)/shard_map/all_to_all | solution.py:175
  65.0 6.0 %all-to-all-start.1 = ((bf16[128,64,128]{2,1,0:T(8,128)(2,1)}), bf16[128,64,128]{2,1,0:T(8,128)(2,1)}, u32[]{:S(2)}, u32[]{:S(2)}) async-start(bf16[128,64,128]{2,1,0:T(8,128)(2,1)} %copy.34), calls=%async_computation.1 | async-start | bytes 4194304 | tf_op jit(solution)/shard_map/all_to_all | solution.py:188
  71.0 2.4 %copy.38 = bf16[4,32,64,128]{3,2,1,0:T(8,128)(2,1)S(1)} copy(bf16[4,32,64,128]{3,1,2,0:T(8,128)(2,1)} %bitcast.14) | data formatting | bytes 4194304 | tf_op jit(solution)/shard_map/all_to_all | solution.py:175
  73.4 3.1 %copy.50 = bf16[16,8,64,128]{3,1,2,0:T(8,128)(2,1)} copy(bf16[16,8,64,128]{3,2,1,0:T(8,128)(2,1)S(1)} %bitcast.69) | data formatting | bytes 4194304
  76.6 3.2 %copy.39 = bf16[8192,128]{1,0:T(8,128)(2,1)S(1)} copy(bf16[8192,128]{0,1:T(8,128)(2,1)} %bitcast.70) | data formatting | bytes 4194304 | tf_op jit(solution)/shard_map/dot_general | solution.py:179
  80.8 1.0 fusion.24
  81.8 1.0 fusion.8
  83.0 2.9 %copy.40 = bf16[128,64,128]{2,1,0:T(8,128)(2,1)} copy(bf16[128,64,128]{0,2,1:T(8,128)(2,1)S(1)} %pad_maximum_fusion.1) | data formatting | bytes 4194304 | tf_op jit(solution)/shard_map/concatenate | solution.py:42
  86.0 33.6 %all-to-all-done.1 = bf16[128,64,128]{2,1,0:T(8,128)(2,1)} async-done(((bf16[128,64,128]{2,1,0:T(8,128)(2,1)}), bf16[128,64,128]{2,1,0:T(8,128)(2,1)}, u32[]{:S(2)}, u32[]{:S(2)}) %all-to-all-start.1) | async-done | bytes 2097184 | tf_op jit(solution)/shard_map/all_to_all | solution.py:188
  119.6 4.1 %all-to-all-start.3 = ((bf16[128,64,128]{2,1,0:T(8,128)(2,1)}), bf16[128,64,128]{2,1,0:T(8,128)(2,1)S(1)}, u32[]{:S(2)}, u32[]{:S(2)}) async-start(bf16[128,64,128]{2,1,0:T(8,128)(2,1)} %copy.40), calls=%async_computation.3 | async-start | bytes 4194304 | tf_op jit(solution)/shard_map/all_to_all | solution.py:188
  125.0 67.3 %all_gather.6 = f32[2,32,64]{2,0,1:T(2,128)S(1)} all-gather(f32[2,4,64]{2,0,1:T(2,128)S(1)} %pad_maximum_fusion.2), channel_id=1, replica_groups=mesh['gx'=8,'ka'=4] {'gx'}, dimensions={1}, use_global_device_ids=true | all-gather | bytes 18432 | tf_op jit(solution)/shard_map/all_gather | solution.py:171
  192.5 3.1 %copy.35 = bf16[4,32,64,128]{3,2,1,0:T(8,128)(2,1)} copy(bf16[4,32,64,128]{3,2,0,1:T(8,128)(2,1)} %bitcast.9) | data formatting | bytes 4194304 | tf_op jit(solution)/shard_map/all_to_all | solution.py:188
  196.1 3.9 %fusion.6 = bf16[4,32,64,128]{3,2,0,1:T(8,128)(2,1)S(1)} fusion(f32[4,32,64,128]{3,2,0,1:T(8,128)S(1)} %convert_element_type.47, f32[4,64]{1,0:T(4,128)S(1)} %divide_multiply_fusion, f32[32,64]{1,0:T(8,128)S(1)} %bitcast.76, f32[32,64]{1,0:T(8,128)S(1)} %bitcast.75), kind=kLoop, calls=%fused_computation.10 | loop fusion | flops 13631488 | bytes 6308864 | tf_op jit(solution)/shard_map/convert_element_type | solution.py:224
  204.1 20.0 %all-reduce.1 = f32[32]{0:T(128)} all-reduce(f32[32]{0:T(128)S(1)} %get-tuple-element.15), channel_id=1, replica_groups=mesh['gx'=8,'ka'=4] {'gx'}, use_global_device_ids=true, to_apply=%add.1 | all-reduce | flops 32 | bytes 256
  (37 shorter events, 9.7 us)
Async XLA Ops:
  4.9 29.9 %all-to-all-start = ((bf16[32,256,128]{2,0,1:T(8,128)(2,1)}), bf16[32,256,128]{2,0,1:T(8,128)(2,1)S(1)}, u32[]{:S(2)}, u32[]{:S(2)}) async-start(bf16[32,256,128]{2,0,1:T(8,128)(2,1)} %bitcast.66), calls=%async_computation | async-start | bytes 4194304 | tf_op jit(solution)/shard_map/all_to_all | solution.py:175
  9.1 30.2 %copy-start.1 = (f32[4,64]{1,0:T(4,128)S(1)}, f32[4,64]{1,0:T(4,128)}, u32[]{:S(2)}) copy-start(f32[4,64]{1,0:T(4,128)} %param.7) | copy-start | bytes 3076
  34.8 30.2 %all-to-all-start.2 = ((bf16[32,256,128]{2,0,1:T(8,128)(2,1)}), bf16[32,256,128]{2,0,1:T(8,128)(2,1)}, u32[]{:S(2)}, u32[]{:S(2)}) async-start(bf16[32,256,128]{2,0,1:T(8,128)(2,1)} %bitcast.11), calls=%async_computation.2 | async-start | bytes 4194304 | tf_op jit(solution)/shard_map/all_to_all | solution.py:175
  65.0 54.6 %all-to-all-start.1 = ((bf16[128,64,128]{2,1,0:T(8,128)(2,1)}), bf16[128,64,128]{2,1,0:T(8,128)(2,1)}, u32[]{:S(2)}, u32[]{:S(2)}) async-start(bf16[128,64,128]{2,1,0:T(8,128)(2,1)} %copy.34), calls=%async_computation.1 | async-start | bytes 4194304 | tf_op jit(solution)/shard_map/all_to_all | solution.py:188
  83.0 40.7 %copy-start.4 = (u32[32]{0:T(128)S(1)}, u32[32]{0:T(128)}, u32[]{:S(2)}) copy-start(u32[32]{0:T(128)} %constant.119) | copy-start | bytes 388
  83.0 42.0 %copy-start.2 = (f32[4,64]{1,0:T(4,128)S(1)}, f32[4,64]{1,0:T(4,128)}, u32[]{:S(2)}) copy-start(f32[4,64]{1,0:T(4,128)} %param.9) | copy-start | bytes 3076
  83.0 42.0 %copy-start.3 = (f32[4,64]{1,0:T(4,128)S(1)}, f32[4,64]{1,0:T(4,128)}, u32[]{:S(2)}) copy-start(f32[4,64]{1,0:T(4,128)} %param.8) | copy-start | bytes 3076
  119.6 76.0 %all-to-all-start.3 = ((bf16[128,64,128]{2,1,0:T(8,128)(2,1)}), bf16[128,64,128]{2,1,0:T(8,128)(2,1)S(1)}, u32[]{:S(2)}, u32[]{:S(2)}) async-start(bf16[128,64,128]{2,1,0:T(8,128)(2,1)} %copy.40), calls=%async_computation.3 | async-start | bytes 4194304 | tf_op jit(solution)/shard_map/all_to_all | solution.py:188
  200.9 1.6 copy-start
where the time goes:
time: 226 us; the launch traced here: 225 us
  blocking collectives  87.4 us (39%)
  waiting for transfers between devices  67.1 us (30%)
  local copies, waits for them, and re-layouts  35.8 us (16%)
  starting transfers between devices  18.8 us (8%)
  other arithmetic  9.44 us (4%)
  matrix products  4.96 us (2%)
    all_gather x1, blocking collectives, by_wavenumber(): fields = lax.all_gather(fields, 'gx', axis=1, tiled=True)  67.3 us
    all_to_all x2, waiting for transfers between devices, scatter_waves(): lax.all_to_all(modes, ('gx', 'ka'), split_axis=0, concat_axis=1, tiled=True)  33.6 us
    all_to_all x2, waiting for transfers between devices, gather_angles(): return lax.all_to_all(flat, 'ka', split_axis=1, concat_axis=0, tiled=True)  33.5 us
    unnamed x1, blocking collectives  20 us
    unnamed x16, local copies, waits for them, and re-layouts  16.4 us
    all_to_all x2, starting transfers between devices, scatter_waves(): lax.all_to_all(modes, ('gx', 'ka'), split_axis=0, concat_axis=1, tiled=True)  10.1 us
    all_to_all x2, starting transfers between devices, gather_angles(): return lax.all_to_all(flat, 'ka', split_axis=1, concat_axis=0, tiled=True)  8.68 us
    dot_general x2, local copies, waits for them, and re-layouts, transform_all(): jnp.dot(cos_table, flattened, preferred_element_type=jnp.float32)  6.43 us
  transfers between devices with their start and end apart: 4, of which 3 were waited for; matrix products, arithmetic and copies ran while one was open for 16% of the time, Pallas kernels for 0%

commit v1 on v0

--- a/solution.py
+++ b/solution.py
@@ -168,7 +168,12 @@
     wave_index = owner * waves_here + row % waves_here - total_angles // 2
     cos_table, sin_table = permuted_tables(total_angles, wave_index)
     fields = jnp.stack([mean_velocity, diffusivity])
-    fields = lax.all_gather(fields, "gx", axis=1, tiled=True)
+    ring = [fields]
+    for hop in range(7):
+        ring.append(lax.ppermute(ring[-1], "gx", [(dev, (dev + 1) % 8) for dev in range(8)]))
+    fields = jnp.roll(
+        jnp.concatenate(ring[::-1], axis=1), (lax.axis_index("gx") + 1) * ring[0].shape[1], axis=1
+    )
 
     def gather_angles(snapshots):
         flat = snapshots.reshape(local_angles, points, columns)

time: 226 us -> 232 us (1.027)
  waiting for transfers between devices: 67.1 us -> 140 us
  blocking collectives: 87.4 us -> 17.6 us
  starting transfers between devices: 18.8 us -> 21.5 us
    ppermute x0 -> x7, waiting for transfers between devices: none -> 73.4 us  [by_wavenumber(): lax.ppermute(ring[-1], 'gx', [(dev, (dev + 1) % 8) for dev in range(8)])]
    all_gather x1 -> x0, blocking collectives: 67.3 us -> none  [by_wavenumber(): fields = lax.all_gather(fields, 'gx', axis=1, tiled=True)]
    ppermute x0 -> x7, starting transfers between devices: none -> 2.69 us  [by_wavenumber(): lax.ppermute(ring[-1], 'gx', [(dev, (dev + 1) % 8) for dev in range(8)])]
    unnamed x1, blocking collectives: 20 us -> 17.6 us
  transfers between devices with their start and end apart: 4 -> 11, of which waited for: 3 -> 10; matrix products, arithmetic and copies ran while one was open for 16% -> 16% of each run, Pallas kernels for 0% -> 0%
where the time goes in v1:
time: 232 us; the launch traced here: 231 us
  waiting for transfers between devices  140 us (60%)
  local copies, waits for them, and re-layouts  36 us (16%)
  starting transfers between devices  21.5 us (9%)
  blocking collectives  17.6 us (8%)
  other arithmetic  9.41 us (4%)
  matrix products  4.97 us (2%)
    ppermute x7, waiting for transfers between devices, by_wavenumber(): lax.ppermute(ring[-1], 'gx', [(dev, (dev + 1) % 8) for dev in range(8)])  73.4 us
    all_to_all x2, waiting for transfers between devices, scatter_waves(): lax.all_to_all(modes, ('gx', 'ka'), split_axis=0, concat_axis=1, tiled=True)  33.7 us
    all_to_all x2, waiting for transfers between devices, gather_angles(): return lax.all_to_all(flat, 'ka', split_axis=1, concat_axis=0, tiled=True)  33.5 us
    unnamed x1, blocking collectives  17.6 us
    unnamed x16, local copies, waits for them, and re-layouts  16.4 us
    all_to_all x2, starting transfers between devices, scatter_waves(): lax.all_to_all(modes, ('gx', 'ka'), split_axis=0, concat_axis=1, tiled=True)  10.1 us
    all_to_all x2, starting transfers between devices, gather_angles(): return lax.all_to_all(flat, 'ka', split_axis=1, concat_axis=0, tiled=True)  8.69 us
    dot_general x2, local copies, waits for them, and re-layouts, transform_all(): jnp.dot(cos_table, flattened, preferred_element_type=jnp.float32)  6.43 us
  transfers between devices with their start and end apart: 11, of which 10 were waited for; matrix products, arithmetic and copies ran while one was open for 16% of the time, Pallas kernels for 0%

profile of v1, /device:TPU:0, one launch (start us, length us, event | category | flops | bytes accessed | tf_op | source)
XLA Modules:
  0.0 231.5 jit_solution(16968181986057173234)
XLA Ops:
  0.6 4.3 %copy.30 = bf16[32,4,64,128]{3,0,2,1:T(8,128)(2,1)} copy(bf16[32,4,64,128]{3,2,1,0:T(8,128)(2,1)} %param.6) | data formatting | bytes 4194304 | tf_op args[1]
  4.9 4.2 %all-to-all-start = ((bf16[32,256,128]{2,0,1:T(8,128)(2,1)}), bf16[32,256,128]{2,0,1:T(8,128)(2,1)S(1)}, u32[]{:S(2)}, u32[]{:S(2)}) async-start(bf16[32,256,128]{2,0,1:T(8,128)(2,1)} %bitcast.68), calls=%async_computation | async-start | bytes 4194304 | tf_op jit(solution)/shard_map/all_to_all | solution.py:180
  9.1 4.3 %copy.36 = bf16[32,4,64,128]{3,0,2,1:T(8,128)(2,1)} copy(bf16[32,4,64,128]{3,2,1,0:T(8,128)(2,1)} %param.5) | data formatting | bytes 4194304 | tf_op args[0]
  13.4 21.4 %all-to-all-done = bf16[32,256,128]{2,0,1:T(8,128)(2,1)S(1)} async-done(((bf16[32,256,128]{2,0,1:T(8,128)(2,1)}), bf16[32,256,128]{2,0,1:T(8,128)(2,1)S(1)}, u32[]{:S(2)}, u32[]{:S(2)}) %all-to-all-start) | async-done | bytes 2097184 | tf_op jit(solution)/shard_map/all_to_all | solution.py:180
  34.8 4.5 %all-to-all-start.2 = ((bf16[32,256,128]{2,0,1:T(8,128)(2,1)}), bf16[32,256,128]{2,0,1:T(8,128)(2,1)}, u32[]{:S(2)}, u32[]{:S(2)}) async-start(bf16[32,256,128]{2,0,1:T(8,128)(2,1)} %bitcast.11), calls=%async_computation.2 | async-start | bytes 4194304 | tf_op jit(solution)/shard_map/all_to_all | solution.py:180
  40.3 3.1 %copy.51 = bf16[16,8,64,128]{3,1,2,0:T(8,128)(2,1)} copy(bf16[16,8,64,128]{3,2,1,0:T(8,128)(2,1)S(1)} %bitcast.69) | data formatting | bytes 4194304
  43.4 3.2 %copy.33 = bf16[8192,128]{1,0:T(8,128)(2,1)S(1)} copy(bf16[8192,128]{0,1:T(8,128)(2,1)} %bitcast.70) | data formatting | bytes 4194304 | tf_op jit(solution)/shard_map/dot_general | solution.py:184
  53.0 12.1 %all-to-all-done.2 = bf16[32,256,128]{2,0,1:T(8,128)(2,1)} async-done(((bf16[32,256,128]{2,0,1:T(8,128)(2,1)}), bf16[32,256,128]{2,0,1:T(8,128)(2,1)}, u32[]{:S(2)}, u32[]{:S(2)}) %all-to-all-start.2) | async-done | bytes 2097184 | tf_op jit(solution)/shard_map/all_to_all | solution.py:180
  65.0 6.0 %all-to-all-start.1 = ((bf16[128,64,128]{2,1,0:T(8,128)(2,1)}), bf16[128,64,128]{2,1,0:T(8,128)(2,1)}, u32[]{:S(2)}, u32[]{:S(2)}) async-start(bf16[128,64,128]{2,1,0:T(8,128)(2,1)} %copy.34), calls=%async_computation.1 | async-start | bytes 4194304 | tf_op jit(solution)/shard_map/all_to_all | solution.py:193
  73.5 3.2 %copy.50 = bf16[16,8,64,128]{3,1,2,0:T(8,128)(2,1)} copy(bf16[16,8,64,128]{3,2,1,0:T(8,128)(2,1)S(1)} %bitcast.71) | data formatting | bytes 4194304
  76.6 3.2 %copy.39 = bf16[8192,128]{1,0:T(8,128)(2,1)S(1)} copy(bf16[8192,128]{0,1:T(8,128)(2,1)} %bitcast.72) | data formatting | bytes 4194304 | tf_op jit(solution)/shard_map/dot_general | solution.py:184
  83.1 2.9 %copy.40 = bf16[128,64,128]{2,1,0:T(8,128)(2,1)} copy(bf16[128,64,128]{0,2,1:T(8,128)(2,1)S(1)} %pad_maximum_fusion.1) | data formatting | bytes 4194304 | tf_op jit(solution)/shard_map/concatenate | solution.py:42
  86.0 33.7 %all-to-all-done.1 = bf16[128,64,128]{2,1,0:T(8,128)(2,1)} async-done(((bf16[128,64,128]{2,1,0:T(8,128)(2,1)}), bf16[128,64,128]{2,1,0:T(8,128)(2,1)}, u32[]{:S(2)}, u32[]{:S(2)}) %all-to-all-start.1) | async-done | bytes 2097184 | tf_op jit(solution)/shard_map/all_to_all | solution.py:193
  119.6 4.1 %all-to-all-start.3 = ((bf16[128,64,128]{2,1,0:T(8,128)(2,1)}), bf16[128,64,128]{2,1,0:T(8,128)(2,1)S(1)}, u32[]{:S(2)}, u32[]{:S(2)}) async-start(bf16[128,64,128]{2,1,0:T(8,128)(2,1)} %copy.40), calls=%async_computation.3 | async-start | bytes 4194304 | tf_op jit(solution)/shard_map/all_to_all | solution.py:193
  125.6 37.7 %collective-permute-done = f32[2,4,64]{2,1,0:T(4,128)S(1)} collective-permute-done((f32[2,4,64]{2,1,0:T(4,128)S(1)}, f32[2,4,64]{2,1,0:T(4,128)S(1)}, u32[]{:S(2)}, u32[]{:S(2)}) %collective-permute-start) | collective-permute-done | bytes 2080 | tf_op jit(solution)/shard_map/ppermute | solution.py:173
  163.2 6.4 %collective-permute-done.1 = f32[2,4,64]{2,1,0:T(4,128)S(1)} collective-permute-done((f32[2,4,64]{2,1,0:T(4,128)S(1)}, f32[2,4,64]{2,1,0:T(4,128)S(1)}, u32[]{:S(2)}, u32[]{:S(2)}) %collective-permute-start.1) | collective-permute-done | bytes 2080 | tf_op jit(solution)/shard_map/ppermute | solution.py:173
  169.6 6.3 %collective-permute-done.2 = f32[2,4,64]{2,1,0:T(4,128)S(1)} collective-permute-done((f32[2,4,64]{2,1,0:T(4,128)S(1)}, f32[2,4,64]{2,1,0:T(4,128)S(1)}, u32[]{:S(2)}, u32[]{:S(2)}) %collective-permute-start.2) | collective-permute-done | bytes 2080 | tf_op jit(solution)/shard_map/ppermute | solution.py:173
  176.8 5.4 %collective-permute-done.3 = f32[2,4,64]{2,1,0:T(4,128)S(1)} collective-permute-done((f32[2,4,64]{2,1,0:T(4,128)S(1)}, f32[2,4,64]{2,1,0:T(4,128)S(1)}, u32[]{:S(2)}, u32[]{:S(2)}) %collective-permute-start.3) | collective-permute-done | bytes 2080 | tf_op jit(solution)/shard_map/ppermute | solution.py:173
  182.3 6.3 %collective-permute-done.4 = f32[2,4,64]{2,1,0:T(4,128)S(1)} collective-permute-done((f32[2,4,64]{2,1,0:T(4,128)S(1)}, f32[2,4,64]{2,1,0:T(4,128)S(1)}, u32[]{:S(2)}, u32[]{:S(2)}) %collective-permute-start.4) | collective-permute-done | bytes 2080 | tf_op jit(solution)/shard_map/ppermute | solution.py:173
  188.6 6.3 %collective-permute-done.5 = f32[2,4,64]{2,1,0:T(4,128)S(1)} collective-permute-done((f32[2,4,64]{2,1,0:T(4,128)S(1)}, f32[2,4,64]{2,1,0:T(4,128)S(1)}, u32[]{:S(2)}, u32[]{:S(2)}) %collective-permute-start.5) | collective-permute-done | bytes 2080 | tf_op jit(solution)/shard_map/ppermute | solution.py:173
  196.2 5.0 %collective-permute-done.6 = f32[2,4,64]{2,1,0:T(4,128)S(1)} collective-permute-done((f32[2,4,64]{2,1,0:T(4,128)S(1)}, f32[2,4,64]{2,1,0:T(4,128)S(1)}, u32[]{:S(2)}, u32[]{:S(2)}) %collective-permute-start.6) | collective-permute-done | bytes 2080 | tf_op jit(solution)/shard_map/ppermute | solution.py:173
  201.3 3.1 %copy.35 = bf16[4,32,64,128]{3,2,1,0:T(8,128)(2,1)} copy(bf16[4,32,64,128]{3,2,0,1:T(8,128)(2,1)} %bitcast.9) | data formatting | bytes 4194304 | tf_op jit(solution)/shard_map/all_to_all | solution.py:193
  204.9 3.9 %fusion.6 = bf16[4,32,64,128]{3,2,0,1:T(8,128)(2,1)S(1)} fusion(f32[4,32,64,128]{3,2,0,1:T(8,128)S(1)} %convert_element_type.47, f32[4,64]{1,0:T(4,128)S(1)} %divide_multiply_fusion, f32[32,64]{1,0:T(8,128)S(1)} %get-tuple-element.12, f32[32,64]{1,0:T(8,128)S(1)} %get-tuple-element.11), kind=kLoop, calls=%fused_computation.10 | loop fusion | flops 13631488 | bytes 6308864 | tf_op jit(solution)/shard_map/convert_element_type | solution.py:229
  213.0 17.6 %all-reduce.1 = f32[32]{0:T(128)} all-reduce(f32[32]{0:T(128)S(1)} %get-tuple-element.15), channel_id=1, replica_groups=mesh['gx'=8,'ka'=4] {'gx'}, use_global_device_ids=true, to_apply=%add.1 | all-reduce | flops 32 | bytes 256
  (51 shorter events, 21.8 us)
Async XLA Ops:
  4.9 29.9 %all-to-all-start = ((bf16[32,256,128]{2,0,1:T(8,128)(2,1)}), bf16[32,256,128]{2,0,1:T(8,128)(2,1)S(1)}, u32[]{:S(2)}, u32[]{:S(2)}) async-start(bf16[32,256,128]{2,0,1:T(8,128)(2,1)} %bitcast.68), calls=%async_computation | async-start | bytes 4194304 | tf_op jit(solution)/shard_map/all_to_all | solution.py:180
  9.1 30.2 %copy-start.1 = (f32[4,64]{1,0:T(4,128)S(1)}, f32[4,64]{1,0:T(4,128)}, u32[]{:S(2)}) copy-start(f32[4,64]{1,0:T(4,128)} %param.7) | copy-start | bytes 3076
  34.8 30.2 %all-to-all-start.2 = ((bf16[32,256,128]{2,0,1:T(8,128)(2,1)}), bf16[32,256,128]{2,0,1:T(8,128)(2,1)}, u32[]{:S(2)}, u32[]{:S(2)}) async-start(bf16[32,256,128]{2,0,1:T(8,128)(2,1)} %bitcast.11), calls=%async_computation.2 | async-start | bytes 4194304 | tf_op jit(solution)/shard_map/all_to_all | solution.py:180
  65.0 54.6 %all-to-all-start.1 = ((bf16[128,64,128]{2,1,0:T(8,128)(2,1)}), bf16[128,64,128]{2,1,0:T(8,128)(2,1)}, u32[]{:S(2)}, u32[]{:S(2)}) async-start(bf16[128,64,128]{2,1,0:T(8,128)(2,1)} %copy.34), calls=%async_computation.1 | async-start | bytes 4194304 | tf_op jit(solution)/shard_map/all_to_all | solution.py:193
  83.0 40.7 %copy-start.2 = (f32[4,64]{1,0:T(4,128)S(1)}, f32[4,64]{1,0:T(4,128)}, u32[]{:S(2)}) copy-start(f32[4,64]{1,0:T(4,128)} %param.9) | copy-start | bytes 3076
  83.0 40.7 %copy-start.3 = (f32[4,64]{1,0:T(4,128)S(1)}, f32[4,64]{1,0:T(4,128)}, u32[]{:S(2)}) copy-start(f32[4,64]{1,0:T(4,128)} %param.8) | copy-start | bytes 3076
  83.0 111.9 %copy-start.4 = (u32[32]{0:T(128)S(1)}, u32[32]{0:T(128)}, u32[]{:S(2)}) copy-start(u32[32]{0:T(128)} %constant.141) | copy-start | bytes 388
  119.6 84.9 %all-to-all-start.3 = ((bf16[128,64,128]{2,1,0:T(8,128)(2,1)}), bf16[128,64,128]{2,1,0:T(8,128)(2,1)S(1)}, u32[]{:S(2)}, u32[]{:S(2)}) async-start(bf16[128,64,128]{2,1,0:T(8,128)(2,1)} %copy.40), calls=%async_computation.3 | async-start | bytes 4194304 | tf_op jit(solution)/shard_map/all_to_all | solution.py:193
  123.8 39.5 %collective-permute-start = (f32[2,4,64]{2,1,0:T(4,128)S(1)}, f32[2,4,64]{2,1,0:T(4,128)S(1)}, u32[]{:S(2)}, u32[]{:S(2)}) collective-permute-start(f32[2,4,64]{2,1,0:T(4,128)S(1)} %pad_maximum_fusion.2), channel_id=1, source_target_pairs={{0,4},{4,8},{8,12},{12,16},{16,20},{20,24},{24,28},{28,0},{1,5},{5... | collective-permute-start | bytes 6152 | tf_op jit(solution)/shard_map/ppermute | solution.py:173
  163.2 6.4 %collective-permute-start.1 = (f32[2,4,64]{2,1,0:T(4,128)S(1)}, f32[2,4,64]{2,1,0:T(4,128)S(1)}, u32[]{:S(2)}, u32[]{:S(2)}) collective-permute-start(f32[2,4,64]{2,1,0:T(4,128)S(1)} %collective-permute-done), channel_id=1, source_target_pairs={{0,4},{4,8},{8,12},{12,16},{16,20},{20,24},{24,28},{28,0},{1,5},{5... | collective-permute-start | bytes 6152 | tf_op jit(solution)/shard_map/ppermute | solution.py:173
  169.6 6.3 %collective-permute-start.2 = (f32[2,4,64]{2,1,0:T(4,128)S(1)}, f32[2,4,64]{2,1,0:T(4,128)S(1)}, u32[]{:S(2)}, u32[]{:S(2)}) collective-permute-start(f32[2,4,64]{2,1,0:T(4,128)S(1)} %collective-permute-done.1), channel_id=1, source_target_pairs={{0,4},{4,8},{8,12},{12,16},{16,20},{20,24},{24,28},{28,0},{1,5},{5... | collective-permute-start | bytes 6152 | tf_op jit(solution)/shard_map/ppermute | solution.py:173
  175.9 6.3 %collective-permute-start.3 = (f32[2,4,64]{2,1,0:T(4,128)S(1)}, f32[2,4,64]{2,1,0:T(4,128)S(1)}, u32[]{:S(2)}, u32[]{:S(2)}) collective-permute-start(f32[2,4,64]{2,1,0:T(4,128)S(1)} %collective-permute-done.2), channel_id=1, source_target_pairs={{0,4},{4,8},{8,12},{12,16},{16,20},{20,24},{24,28},{28,0},{1,5},{5... | collective-permute-start | bytes 6152 | tf_op jit(solution)/shard_map/ppermute | solution.py:173
  182.3 6.3 %collective-permute-start.4 = (f32[2,4,64]{2,1,0:T(4,128)S(1)}, f32[2,4,64]{2,1,0:T(4,128)S(1)}, u32[]{:S(2)}, u32[]{:S(2)}) collective-permute-start(f32[2,4,64]{2,1,0:T(4,128)S(1)} %collective-permute-done.3), channel_id=1, source_target_pairs={{0,4},{4,8},{8,12},{12,16},{16,20},{20,24},{24,28},{28,0},{1,5},{5... | collective-permute-start | bytes 6152 | tf_op jit(solution)/shard_map/ppermute | solution.py:173
  188.6 6.3 %collective-permute-start.5 = (f32[2,4,64]{2,1,0:T(4,128)S(1)}, f32[2,4,64]{2,1,0:T(4,128)S(1)}, u32[]{:S(2)}, u32[]{:S(2)}) collective-permute-start(f32[2,4,64]{2,1,0:T(4,128)S(1)} %collective-permute-done.4), channel_id=1, source_target_pairs={{0,4},{4,8},{8,12},{12,16},{16,20},{20,24},{24,28},{28,0},{1,5},{5... | collective-permute-start | bytes 6152 | tf_op jit(solution)/shard_map/ppermute | solution.py:173
  194.9 6.3 %collective-permute-start.6 = (f32[2,4,64]{2,1,0:T(4,128)S(1)}, f32[2,4,64]{2,1,0:T(4,128)S(1)}, u32[]{:S(2)}, u32[]{:S(2)}) collective-permute-start(f32[2,4,64]{2,1,0:T(4,128)S(1)} %collective-permute-done.5), channel_id=1, source_target_pairs={{0,4},{4,8},{8,12},{12,16},{16,20},{20,24},{24,28},{28,0},{1,5},{5... | collective-permute-start | bytes 6152 | tf_op jit(solution)/shard_map/ppermute | solution.py:173
  209.8 1.6 copy-start
